TPU v7x, 256 devices: a whole 4x4x8 slice. The times are simulated.
256 devices in a mesh: rep: 32 (over z, y_hi, core), tp: 8 (over x, y_lo).
Axes of the slice: x: 4, y: 4 (y_hi: 2, y_lo: 2; y = y_hi * 2 + y_lo), z: 8, core: 2. Of those that a mesh axis runs over, the one named last changes fastest.
Arguments:
- acts: bfloat16 [32, 1024, 4096], P('rep', 'tp'), may hold values from -6 to 6
- weights: bfloat16 [32, 4096, 4096], P('rep', None, 'tp'), may hold values from -6 to 6
- cotangent: bfloat16 [32, 1024, 4096], P('rep', None, 'tp'), may hold values from -6 to 6
- start_factors: float32 [4096, 32], replicated, may hold values from -6 to 6
Outputs:
- projected: bfloat16 [32, 1024, 4096], P('rep', None, 'tp')
- new_weights: bfloat16 [32, 4096, 4096], P('rep', None, 'tp')
All inputs are finite; a program needn't handle non-finite values.
Results may differ from a plain program's by a relative error of at most 0.001.
Values may be sent and summed in bfloat16 or wider, within the bound.
No kernel may reach another device: no remote copies, remote signals or barrier semaphores. Data moves between devices by JAX's collectives and lax.ppermute only.
A program may use at most 128 MiB of HBM per device.

v0:
```python
import jax
import jax.numpy as jnp
from jax import lax
from jax.sharding import PartitionSpec as P

D = 4096
STEPS = 3
HIGH = lax.Precision.HIGHEST


def partner(block, axis, stride):
    count = lax.axis_size(axis)
    route = []
    for low in range(count):
        high = low | 1 << stride
        if high != low and high < count:
            route += [(low, high), (high, low)]
    return lax.ppermute(block, axis, route)


def shards(acts, weights, cotangent, start_factors):
    scale = D ** (-0.5)
    weight_part = weights[0]
    grad_out = cotangent[0]
    projected = (
        jnp.dot(
            lax.all_gather(acts, "tp", axis=1, tiled=True)[0],
            weight_part,
            preferred_element_type=jnp.float32,
        )
        * scale
    ).astype(jnp.bfloat16)[None]
    grad = lax.dot_general(
        lax.all_gather(acts, "tp", axis=1, tiled=True)[0],
        grad_out,
        (((0,), (0,)), ((), ())),
        preferred_element_type=jnp.float32,
    )
    current = weight_part.astype(jnp.float32) - 0.5 * scale * grad
    for step in range(STEPS):
        side = lax.dot_general(current, start_factors, (((0,), (0,)), ((), ())), precision=HIGH)
        other = partner(side, "rep", step)
        diff = side - other
        gram = lax.psum(jnp.dot(diff.T, diff, precision=HIGH), "tp")
        lower = jnp.linalg.cholesky(gram)
        ortho = jax.scipy.linalg.solve_triangular(lower, diff.T, lower=True).T
        local = jnp.dot(current, ortho, precision=HIGH)
        summed = lax.psum(local, "tp")
        back = summed + partner(summed, "rep", step)
        current = current - 0.5 * jnp.dot(back, ortho.T, precision=HIGH)
    return (projected, current.astype(jnp.bfloat16)[None])


def solution(mesh):
    in_specs = (P("rep", "tp", None), P("rep", None, "tp"), P("rep", None, "tp"), P())
    out_specs = (P("rep", None, "tp"), P("rep", None, "tp"))
    return jax.shard_map(shards, mesh=mesh, in_specs=in_specs, out_specs=out_specs, check_vma=False)
```

profile of v0, /device:TPU:16, one launch (start us, length us, event | category | flops | bytes accessed | tf_op | source)
XLA Modules:
  0.0 682.2 jit_solution(12295986545836351096)
XLA Ops:
  7.2 0.7 all-gather.2.cloned.1.call-update
  8.0 175.2 %all-gather.2.cloned.1.call-done = bf16[1,1024,4096]{2,1,0:T(8,128)(2,1)} async-done(((bf16[1,128,4096]{2,1,0:T(8,128)(2,1)}), bf16[1,1024,4096]{2,1,0:T(8,128)(2,1)}) %all-gather.2.cloned.1.call-update) | async-done | bytes 8388624 | tf_op jit(solution)/shard_map/all_gather | solution.py:27
  183.2 12.2 %multiply_subtract_fusion.2 = f32[4096,512]{1,0:T(8,128)S(1)} fusion(bf16[1,1024,4096]{2,1,0:T(8,128)(2,1)} %all-gather.2.cloned.1.call-done, bf16[1,4096,512]{2,1,0:T(8,128)(2,1)} %param.8, bf16[1,1024,512]{2,1,0:T(8,128)(2,1)S(1)} %copy-done), kind=kOutput, calls=%fused_computation.7 | convolution fusion | flops 4301258752 | bytes 22020096 | tf_op jit(solution)/shard_map/dot_general | solution.py:33
  195.4 3.2 copy-done.3
  198.6 5.1 fusion.45
  203.8 1.2 collective-permute-done
  205.0 0.2 fusion.34
  205.2 34.0 %psum.42 = f32[32,32]{0,1:T(8,128)S(1)} all-reduce(f32[32,32]{0,1:T(8,128)S(1)} %fusion.34), channel_id=1, replica_groups=mesh['rep'=32,'tp'=8] {'tp'}, use_global_device_ids=true, to_apply=%region_0.0 | all-reduce | flops 1024 | bytes 8192 | tf_op jit(solution)/shard_map/psum | solution.py:44
  239.4 2.9 cholesky.59
  242.3 0.6 compare_reduce_fusion.2
  243.0 0.7 fusion.36
  243.6 2.4 custom-call.7
  246.0 0.3 fusion.25
  246.3 10.8 %fusion.46 = f32[4096,32]{0,1:T(8,128)} fusion(f32[4096,512]{1,0:T(8,128)} %copy-done.3, f32[32,512]{1,0:T(8,128)S(1)} %fusion.25), kind=kOutput, calls=%fused_computation.55 | convolution fusion | flops 805306368 | bytes 8978432 | tf_op jit(solution)/shard_map/dot_general | solution.py:47
  257.2 78.7 %all-reduce.4.cloned.1.call-done = f32[4096,32]{0,1:T(8,128)} async-done(((f32[4096,32]{0,1:T(8,128)}), f32[4096,32]{0,1:T(8,128)}) %all-reduce.4.cloned.1.call-update) | async-done | bytes 524304 | tf_op jit(solution)/shard_map/psum | solution.py:48
  335.9 2.1 collective-permute-done.1
  338.0 9.4 %multiply_subtract_fusion.1 = f32[4096,512]{1,0:T(8,128)S(1)} fusion(f32[4096,512]{1,0:T(8,128)} %copy-done.3, f32[32,512]{1,0:T(8,128)S(1)} %fusion.25, f32[4096,32]{0,1:T(8,128)} %all-reduce.4.cloned.1.call-done, f32[4096,32]{0,1:T(8,128)S(1)} %collective-permute-done.1), kind=kOutput, calls=%fused_computation.6 | convolution fusion | flops 809631744 | bytes 17891328 | tf_op jit(solution)/shard_map/dot_general | solution.py:50
  347.4 3.2 copy-done.1
  350.6 5.1 fusion.47
  355.7 1.0 collective-permute-start.2
  356.7 4.9 collective-permute-done.2
  361.6 0.2 fusion.31
  361.8 32.4 %psum.44 = f32[32,32]{0,1:T(8,128)S(1)} all-reduce(f32[32,32]{0,1:T(8,128)S(1)} %fusion.31), channel_id=1, replica_groups=mesh['rep'=32,'tp'=8] {'tp'}, use_global_device_ids=true, to_apply=%region_4.0 | all-reduce | flops 1024 | bytes 8192 | tf_op jit(solution)/shard_map/psum | solution.py:44
  394.3 2.9 cholesky.70
  397.2 0.6 compare_reduce_fusion.1
  397.9 0.7 fusion.37
  398.5 2.4 custom-call.8
  401.0 0.3 fusion.23
  401.3 10.8 %fusion.48 = f32[4096,32]{0,1:T(8,128)} fusion(f32[4096,512]{1,0:T(8,128)} %copy-done.1, f32[32,512]{1,0:T(8,128)S(1)} %fusion.23), kind=kOutput, calls=%fused_computation.57 | convolution fusion | flops 805306368 | bytes 8978432 | tf_op jit(solution)/shard_map/dot_general | solution.py:47
  412.1 78.8 %all-reduce.6.cloned.1.call-done = f32[4096,32]{0,1:T(8,128)} async-done(((f32[4096,32]{0,1:T(8,128)}), f32[4096,32]{0,1:T(8,128)}) %all-reduce.6.cloned.1.call-update) | async-done | bytes 524304 | tf_op jit(solution)/shard_map/psum | solution.py:48
  490.9 0.9 collective-permute-start.3
  491.8 10.0 %collective-permute-done.3 = f32[4096,32]{0,1:T(8,128)S(1)} collective-permute-done((f32[4096,32]{0,1:T(8,128)}, f32[4096,32]{0,1:T(8,128)S(1)}, u32[]{:S(2)}, u32[]{:S(2)}) %collective-permute-start.3) | collective-permute-done | bytes 524320 | tf_op jit(solution)/shard_map/ppermute | solution.py:18
  501.8 9.4 %multiply_subtract_fusion = f32[4096,512]{1,0:T(8,128)S(1)} fusion(f32[4096,512]{1,0:T(8,128)} %copy-done.1, f32[32,512]{1,0:T(8,128)S(1)} %fusion.23, f32[4096,32]{0,1:T(8,128)} %all-reduce.6.cloned.1.call-done, f32[4096,32]{0,1:T(8,128)S(1)} %collective-permute-done.3), kind=kOutput, calls=%fused_computation.5 | convolution fusion | flops 809631744 | bytes 17891328 | tf_op jit(solution)/shard_map/dot_general | solution.py:50
  511.3 3.2 copy-done.2
  514.5 5.1 fusion.49
  519.5 1.6 collective-permute-start.4
  521.2 2.7 collective-permute-done.4
  524.1 32.5 %psum.46 = f32[32,32]{0,1:T(8,128)S(1)} all-reduce(f32[32,32]{0,1:T(8,128)S(1)} %fusion.28), channel_id=1, replica_groups=mesh['rep'=32,'tp'=8] {'tp'}, use_global_device_ids=true, to_apply=%region_6.9 | all-reduce | flops 1024 | bytes 8192 | tf_op jit(solution)/shard_map/psum | solution.py:44
  556.7 2.9 cholesky.81
  559.6 0.6 compare_reduce_fusion
  560.2 0.7 fusion.38
  560.9 2.4 custom-call.9
  563.3 0.3 fusion.21
  563.6 10.8 %fusion.50 = f32[4096,32]{0,1:T(8,128)} fusion(f32[4096,512]{1,0:T(8,128)} %copy-done.2, f32[32,512]{1,0:T(8,128)S(1)} %fusion.21), kind=kOutput, calls=%fused_computation.59 | convolution fusion | flops 805306368 | bytes 8978432 | tf_op jit(solution)/shard_map/dot_general | solution.py:47
  574.4 78.8 %all-reduce.8.cloned.1.call-done = f32[4096,32]{0,1:T(8,128)} async-done(((f32[4096,32]{0,1:T(8,128)}), f32[4096,32]{0,1:T(8,128)}) %all-reduce.8.cloned.1.call-update) | async-done | bytes 524304 | tf_op jit(solution)/shard_map/psum | solution.py:48
  653.2 1.6 collective-permute-start.5
  654.8 10.0 %fusion.12 = bf16[1,1024,512]{2,1,0:T(8,128)(2,1)} fusion(bf16[1,4096,512]{2,1,0:T(8,128)(2,1)} %param.8, bf16[1,1024,4096]{2,1,0:T(8,128)(2,1)} %all-gather.2.cloned.1.call-done), kind=kOutput, calls=%fused_computation.11 | convolution fusion | flops 4296015872 | bytes 13631488 | tf_op jit(solution)/shard_map/dot_general | solution.py:26
  664.8 10.6 %fusion.6 = bf16[1,4096,512]{2,1,0:T(8,128)(2,1)} fusion(f32[4096,512]{1,0:T(8,128)} %copy-done.2, f32[32,512]{1,0:T(8,128)S(1)} %fusion.21, f32[4096,32]{0,1:T(8,128)S(1)} %copy-done.5, f32[4096,32]{0,1:T(8,128)S(1)} %collective-permute-done.5), kind=kOutput, calls=%fused_computation.8 | convolution fusion | flops 811728896 | bytes 13697024 | tf_op jit(solution)/shard_map/dot_general | solution.py:50
  (29 shorter events, 0.9 us)
Async XLA Ops:
  7.2 176.0 %copy-start = (bf16[1,1024,512]{2,1,0:T(8,128)(2,1)S(1)}, bf16[1,1024,512]{2,1,0:T(8,128)(2,1)}, u32[]{:S(2)}) copy-start(bf16[1,1024,512]{2,1,0:T(8,128)(2,1)} %param.9) | copy-start | bytes 3145732
  7.2 176.0 %all-gather.2.cloned.1.call-start = ((), (), s32[]{:S(2)}) async-start(), calls=%async_computation | async-start | bytes 9437184 | tf_op jit(solution)/shard_map/all_gather | solution.py:27
  7.9 190.7 %copy-start.4 = (f32[4096,32]{0,1:T(8,128)S(1)}, f32[4096,32]{0,1:T(8,128)}, u32[]{:S(2)}) copy-start(f32[4096,32]{0,1:T(8,128)} %param.10) | copy-start | bytes 1572868
  7.9 328.0 %all-reduce.4.cloned.1.call-start = ((), (), s32[]{:S(2)}) async-start(), calls=%async_computation.1 | async-start | bytes 1048576 | tf_op jit(solution)/shard_map/psum | solution.py:48
  195.4 3.2 copy-start.3
  203.7 1.3 collective-permute-start
  257.1 233.8 %all-reduce.6.cloned.1.call-start = ((), (), s32[]{:S(2)}) async-start(), calls=%async_computation.2 | async-start | bytes 1048576 | tf_op jit(solution)/shard_map/psum | solution.py:48
  335.9 2.1 collective-permute-start.1
  347.4 3.2 copy-start.1
  355.7 5.9 collective-permute-start.2
  412.1 241.1 %all-reduce.8.cloned.1.call-start = ((), (), s32[]{:S(2)}) async-start(), calls=%async_computation.3 | async-start | bytes 1048576 | tf_op jit(solution)/shard_map/psum | solution.py:48
  490.9 10.9 %collective-permute-start.3 = (f32[4096,32]{0,1:T(8,128)}, f32[4096,32]{0,1:T(8,128)S(1)}, u32[]{:S(2)}, u32[]{:S(2)}) collective-permute-start(f32[4096,32]{0,1:T(8,128)} %all-reduce.6.cloned.1.call-done), channel_id=1, source_target_pairs={{0,16},{16,0},{8,24},{24,8},{32,48},{48,32},{40,56},{56,40},{64,80... | collective-permute-start | bytes 1572872 | tf_op jit(solution)/shard_map/ppermute | solution.py:18
  511.3 3.2 copy-start.2
  519.5 4.4 collective-permute-start.4
  653.2 11.6 %copy-start.5 = (f32[4096,32]{0,1:T(8,128)S(1)}, f32[4096,32]{0,1:T(8,128)}, u32[]{:S(2)}) copy-start(f32[4096,32]{0,1:T(8,128)} %all-reduce.8.cloned.1.call-done) | copy-start | bytes 1572868
  653.2 11.6 %collective-permute-start.5 = (f32[4096,32]{0,1:T(8,128)}, f32[4096,32]{0,1:T(8,128)S(1)}, u32[]{:S(2)}, u32[]{:S(2)}) collective-permute-start(f32[4096,32]{0,1:T(8,128)} %all-reduce.8.cloned.1.call-done), channel_id=1, source_target_pairs={{0,32},{32,0},{8,40},{40,8},{16,48},{48,16},{24,56},{56,24},{64,96... | collective-permute-start | bytes 1572872 | tf_op jit(solution)/shard_map/ppermute | solution.py:18
Sparse Core Ops, SparseCore 0:
  9.8 173.3 all-gather.1
  257.3 78.5 all-reduce.3
  412.2 78.7 all-reduce.5
  574.6 78.6 all-reduce.7
where the time goes:
time: 689 us; the launch traced here: 682 us
  waiting for transfers between devices  433 us (63%)
  matrix products  101 us (15%)
  blocking collectives  98.9 us (14%)
  other arithmetic  20.1 us (3%)
  between operations  14.2 us (2%)
  local copies, waits for them, and re-layouts  9.85 us (1%)
    psum x3, waiting for transfers between devices, shards(): summed = lax.psum(local, 'tp')  236 us
    all_gather x1, waiting for transfers between devices, shards(): lax.all_gather(acts, 'tp', axis=1, tiled=True)[0]  175 us
    psum x3, blocking collectives, shards(): gram = lax.psum(jnp.dot(diff.T, diff, precision=HIGH), 'tp')  98.9 us
    dot_general x3, matrix products, shards(): local = jnp.dot(current, ortho, precision=HIGH)  32.3 us
    dot_general x3, matrix products, shards(): current = current - 0.5 * jnp.dot(back, ortho.T, precision=HIGH)  29.5 us
    ppermute x6, waiting for transfers between devices, partner(): return lax.ppermute(block, axis, route)  21 us
    dot_general x3, matrix products, shards(): lax.dot_general(current, start_factors, (((0,), (0,)), ((), ())), precisi...  15.2 us
  transfers between devices with their start and end apart: 10, of which 9 were waited for; matrix products, arithmetic and copies ran while one was open for 1% of the time, Pallas kernels for 0%

commit v1 on v0

--- a/solution.py
+++ b/solution.py
@@ -6,6 +6,12 @@
 D = 4096
 STEPS = 3
 HIGH = lax.Precision.HIGHEST
+_link_scenes = lambda array_here: jnp.concatenate(
+    lax.all_to_all(
+        jnp.stack([array_here] * lax.axis_size("tp")), "tp", split_axis=0, concat_axis=0
+    ),
+    axis=1,
+)
 
 
 def partner(block, axis, stride):
@@ -23,12 +29,7 @@
     weight_part = weights[0]
     grad_out = cotangent[0]
     projected = (
-        jnp.dot(
-            lax.all_gather(acts, "tp", axis=1, tiled=True)[0],
-            weight_part,
-            preferred_element_type=jnp.float32,
-        )
-        * scale
+        jnp.dot(_link_scenes(acts)[0], weight_part, preferred_element_type=jnp.float32) * scale
     ).astype(jnp.bfloat16)[None]
     grad = lax.dot_general(
         lax.all_gather(acts, "tp", axis=1, tiled=True)[0],

time: 689 us -> 781 us (1.13)
  waiting for transfers between devices: 433 us -> 478 us
  blocking collectives: 98.9 us -> 136 us
    ppermute x6, waiting for transfers between devices: 21 us -> 66.1 us  [partner(): return lax.ppermute(block, axis, route)]
    psum x3, blocking collectives: 98.9 us -> 136 us  [shards(): gram = lax.psum(jnp.dot(diff.T, diff, precision=HIGH), 'tp')]
  transfers between devices with their start and end apart: 10 -> 11, of which waited for: 9 -> 8; matrix products, arithmetic and copies ran while one was open for 1% -> 10% of each run, Pallas kernels for 0% -> 0%
where the time goes in v1:
time: 781 us; the launch traced here: 774 us
  waiting for transfers between devices  478 us (61%)
  blocking collectives  136 us (17%)
  matrix products  101 us (13%)
  other arithmetic  20.1 us (3%)
  local copies, waits for them, and re-layouts  14.2 us (2%)
  between operations  14.2 us (2%)
  starting transfers between devices  10.9 us (1%)
    psum x3, waiting for transfers between devices, shards(): summed = lax.psum(local, 'tp')  236 us
    all_gather x1, waiting for transfers between devices, shards(): lax.all_gather(acts, 'tp', axis=1, tiled=True)[0]  175 us
    psum x3, blocking collectives, shards(): gram = lax.psum(jnp.dot(diff.T, diff, precision=HIGH), 'tp')  136 us
    ppermute x6, waiting for transfers between devices, partner(): return lax.ppermute(block, axis, route)  66.1 us
    dot_general x3, matrix products, shards(): local = jnp.dot(current, ortho, precision=HIGH)  32.3 us
    dot_general x3, matrix products, shards(): current = current - 0.5 * jnp.dot(back, ortho.T, precision=HIGH)  29.4 us
  transfers between devices with their start and end apart: 11, of which 8 were waited for; matrix products, arithmetic and copies ran while one was open for 10% of the time, Pallas kernels for 0%

profile of v1, /device:TPU:16, one launch (start us, length us, event | category | flops | bytes accessed | tf_op | source)
XLA Modules:
  0.0 773.9 jit_solution(17589106683952813086)
XLA Ops:
  7.2 0.7 all-gather.2.cloned.1.call-update
  8.0 175.2 %all-gather.2.cloned.1.call-done = bf16[1,1024,4096]{2,1,0:T(8,128)(2,1)} async-done(((bf16[1,128,4096]{2,1,0:T(8,128)(2,1)}), bf16[1,1024,4096]{2,1,0:T(8,128)(2,1)}) %all-gather.2.cloned.1.call-update) | async-done | bytes 8388624 | tf_op jit(solution)/shard_map/all_gather | solution.py:35
  183.2 12.2 %multiply_subtract_fusion.2 = f32[4096,512]{1,0:T(8,128)S(1)} fusion(bf16[1,1024,4096]{2,1,0:T(8,128)(2,1)} %all-gather.2.cloned.1.call-done, bf16[1,4096,512]{2,1,0:T(8,128)(2,1)} %param.8, bf16[1,1024,512]{2,1,0:T(8,128)(2,1)S(1)} %copy-done), kind=kOutput, calls=%fused_computation.5 | convolution fusion | flops 4301258752 | bytes 22020096 | tf_op jit(solution)/shard_map/dot_general | solution.py:34
  195.4 3.2 copy-done.4
  198.6 5.1 fusion.40
  203.8 1.2 collective-permute-done
  205.2 33.9 %psum.42 = f32[32,32]{0,1:T(8,128)S(1)} all-reduce(f32[32,32]{0,1:T(8,128)S(1)} %fusion.29), channel_id=1, replica_groups=mesh['rep'=32,'tp'=8] {'tp'}, use_global_device_ids=true, to_apply=%region_0.0 | all-reduce | flops 1024 | bytes 8192 | tf_op jit(solution)/shard_map/psum | solution.py:45
  239.2 2.9 cholesky.59
  242.1 0.6 compare_reduce_fusion.2
  242.8 0.7 fusion.31
  243.5 2.4 custom-call.7
  245.9 0.3 fusion.20
  246.2 10.8 %fusion.41 = f32[4096,32]{0,1:T(8,128)} fusion(f32[4096,512]{1,0:T(8,128)} %copy-done.4, f32[32,512]{1,0:T(8,128)S(1)} %fusion.20), kind=kOutput, calls=%fused_computation.54 | convolution fusion | flops 805306368 | bytes 8978432 | tf_op jit(solution)/shard_map/dot_general | solution.py:48
  257.0 78.7 %all-reduce.4.cloned.1.call-done = f32[4096,32]{0,1:T(8,128)} async-done(((f32[4096,32]{0,1:T(8,128)}), f32[4096,32]{0,1:T(8,128)}) %all-reduce.4.cloned.1.call-update) | async-done | bytes 524304 | tf_op jit(solution)/shard_map/psum | solution.py:49
  335.7 4.3 stack.2
  340.0 5.1 all-to-all-start
  345.1 0.6 all-reduce.6.cloned.1.call-start
  345.7 9.3 %multiply_subtract_fusion.1 = f32[4096,512]{1,0:T(8,128)S(1)} fusion(f32[4096,512]{1,0:T(8,128)} %copy-done.4, f32[32,512]{1,0:T(8,128)S(1)} %fusion.20, f32[4096,32]{0,1:T(8,128)S(1)} %copy-done.7, f32[4096,32]{0,1:T(8,128)S(1)} %collective-permute-done.1), kind=kOutput, calls=%fused_computation.4 | convolution fusion | flops 809631744 | bytes 17891328 | tf_op jit(solution)/shard_map/dot_general | solution.py:51
  355.0 3.2 copy-done.3
  358.2 5.1 fusion.42
  363.3 0.9 collective-permute-start.2
  364.2 52.1 %collective-permute-done.2 = f32[512,32]{0,1:T(8,128)S(1)} collective-permute-done((f32[512,32]{0,1:T(8,128)S(1)}, f32[512,32]{0,1:T(8,128)S(1)}, u32[]{:S(2)}, u32[]{:S(2)}) %collective-permute-start.2) | collective-permute-done | bytes 65568 | tf_op jit(solution)/shard_map/ppermute | solution.py:24
  416.5 69.3 %psum.44 = f32[32,32]{0,1:T(8,128)S(1)} all-reduce(f32[32,32]{0,1:T(8,128)S(1)} %fusion.26), channel_id=1, replica_groups=mesh['rep'=32,'tp'=8] {'tp'}, use_global_device_ids=true, to_apply=%region_4.0 | all-reduce | flops 1024 | bytes 8192 | tf_op jit(solution)/shard_map/psum | solution.py:45
  485.9 2.9 cholesky.70
  488.8 0.6 compare_reduce_fusion.1
  489.5 0.7 fusion.32
  490.1 2.4 custom-call.8
  492.6 0.3 fusion.18
  492.9 10.8 %fusion.43 = f32[4096,32]{0,1:T(8,128)} fusion(f32[4096,512]{1,0:T(8,128)} %copy-done.3, f32[32,512]{1,0:T(8,128)S(1)} %fusion.18), kind=kOutput, calls=%fused_computation.56 | convolution fusion | flops 805306368 | bytes 8978432 | tf_op jit(solution)/shard_map/dot_general | solution.py:48
  503.7 78.9 %all-reduce.6.cloned.1.call-done = f32[4096,32]{0,1:T(8,128)} async-done(((f32[4096,32]{0,1:T(8,128)}), f32[4096,32]{0,1:T(8,128)}) %all-reduce.6.cloned.1.call-update) | async-done | bytes 524304 | tf_op jit(solution)/shard_map/psum | solution.py:49
  582.6 0.9 collective-permute-start.3
  583.4 10.0 %collective-permute-done.3 = f32[4096,32]{0,1:T(8,128)S(1)} collective-permute-done((f32[4096,32]{0,1:T(8,128)}, f32[4096,32]{0,1:T(8,128)S(1)}, u32[]{:S(2)}, u32[]{:S(2)}) %collective-permute-start.3) | collective-permute-done | bytes 524320 | tf_op jit(solution)/shard_map/ppermute | solution.py:24
  593.5 9.4 %multiply_subtract_fusion = f32[4096,512]{1,0:T(8,128)S(1)} fusion(f32[4096,512]{1,0:T(8,128)} %copy-done.3, f32[32,512]{1,0:T(8,128)S(1)} %fusion.18, f32[4096,32]{0,1:T(8,128)} %all-reduce.6.cloned.1.call-done, f32[4096,32]{0,1:T(8,128)S(1)} %collective-permute-done.3), kind=kOutput, calls=%fused_computation.3 | convolution fusion | flops 809631744 | bytes 17891328 | tf_op jit(solution)/shard_map/dot_general | solution.py:51
  602.9 3.2 copy-done.2
  606.1 5.1 fusion.44
  611.2 1.6 collective-permute-start.4
  612.8 2.7 collective-permute-done.4
  615.7 32.5 %psum.46 = f32[32,32]{0,1:T(8,128)S(1)} all-reduce(f32[32,32]{0,1:T(8,128)S(1)} %fusion.23), channel_id=1, replica_groups=mesh['rep'=32,'tp'=8] {'tp'}, use_global_device_ids=true, to_apply=%region_6.9 | all-reduce | flops 1024 | bytes 8192 | tf_op jit(solution)/shard_map/psum | solution.py:45
  648.3 2.9 cholesky.81
  651.2 0.6 compare_reduce_fusion
  651.9 0.7 fusion.33
  652.5 2.4 custom-call.9
  655.0 0.3 fusion.16
  655.3 10.8 %fusion.45 = f32[4096,32]{0,1:T(8,128)} fusion(f32[4096,512]{1,0:T(8,128)} %copy-done.2, f32[32,512]{1,0:T(8,128)S(1)} %fusion.16), kind=kOutput, calls=%fused_computation.58 | convolution fusion | flops 805306368 | bytes 8978432 | tf_op jit(solution)/shard_map/dot_general | solution.py:48
  666.1 78.8 %all-reduce.8.cloned.1.call-done = f32[4096,32]{0,1:T(8,128)} async-done(((f32[4096,32]{0,1:T(8,128)}), f32[4096,32]{0,1:T(8,128)}) %all-reduce.8.cloned.1.call-update) | async-done | bytes 524304 | tf_op jit(solution)/shard_map/psum | solution.py:49
  744.8 1.6 collective-permute-start.5
  746.4 10.1 %fusion.9 = bf16[1,1024,512]{2,1,0:T(8,128)(2,1)} fusion(bf16[1024,4096]{1,0:T(8,128)(2,1)} %bitcast.1, bf16[1,4096,512]{2,1,0:T(8,128)(2,1)} %param.8), kind=kOutput, calls=%fused_computation.10 | convolution fusion | flops 4296015872 | bytes 13631488 | tf_op jit(solution)/shard_map/dot_general | solution.py:32
  756.5 10.6 %fusion.4 = bf16[1,4096,512]{2,1,0:T(8,128)(2,1)} fusion(f32[4096,512]{1,0:T(8,128)} %copy-done.2, f32[32,512]{1,0:T(8,128)S(1)} %fusion.16, f32[4096,32]{0,1:T(8,128)S(1)} %copy-done.8, f32[4096,32]{0,1:T(8,128)S(1)} %collective-permute-done.5), kind=kOutput, calls=%fused_computation.6 | convolution fusion | flops 811728896 | bytes 13697024 | tf_op jit(solution)/shard_map/dot_general | solution.py:51
  (38 shorter events, 1.2 us)
Async XLA Ops:
  7.2 176.0 %copy-start = (bf16[1,1024,512]{2,1,0:T(8,128)(2,1)S(1)}, bf16[1,1024,512]{2,1,0:T(8,128)(2,1)}, u32[]{:S(2)}) copy-start(bf16[1,1024,512]{2,1,0:T(8,128)(2,1)} %param.9) | copy-start | bytes 3145732
  7.2 176.0 %all-gather.2.cloned.1.call-start = ((), (), s32[]{:S(2)}) async-start(), calls=%async_computation.1 | async-start | bytes 9437184 | tf_op jit(solution)/shard_map/all_gather | solution.py:35
  7.9 190.7 %copy-start.5 = (f32[4096,32]{0,1:T(8,128)S(1)}, f32[4096,32]{0,1:T(8,128)}, u32[]{:S(2)}) copy-start(f32[4096,32]{0,1:T(8,128)} %param.10) | copy-start | bytes 1572868
  7.9 327.8 %all-reduce.4.cloned.1.call-start = ((), (), s32[]{:S(2)}) async-start(), calls=%async_computation.2 | async-start | bytes 1048576 | tf_op jit(solution)/shard_map/psum | solution.py:49
  195.4 3.2 copy-start.4
  198.6 137.1 %copy-start.6 = (bf16[1,128,4096]{2,1,0:T(8,128)(2,1)S(1)}, bf16[1,128,4096]{2,1,0:T(8,128)(2,1)}, u32[]{:S(2)}) copy-start(bf16[1,128,4096]{2,1,0:T(8,128)(2,1)} %param.7) | copy-start | bytes 3145732
  203.7 1.3 collective-permute-start
  335.7 9.9 %collective-permute-start.1 = (f32[4096,32]{0,1:T(8,128)}, f32[4096,32]{0,1:T(8,128)S(1)}, u32[]{:S(2)}, u32[]{:S(2)}) collective-permute-start(f32[4096,32]{0,1:T(8,128)} %all-reduce.4.cloned.1.call-done), channel_id=1, source_target_pairs={{0,8},{8,0},{16,24},{24,16},{32,40},{40,32},{48,56},{56,48},{64,72... | collective-permute-start | bytes 1572872 | tf_op jit(solution)/shard_map/ppermute | solution.py:24
  340.0 5.7 copy-start.7
  340.0 406.4 %all-to-all-start = ((bf16[8,1,128,4096]{3,2,1,0:T(8,128)(2,1)}), bf16[8,1,128,4096]{3,2,1,0:T(8,128)(2,1)}, u32[]{:S(2)}, u32[]{:S(2)}) async-start(bf16[8,1,128,4096]{3,2,1,0:T(8,128)(2,1)} %stack.2), calls=%async_computation | async-start | bytes 16777216 | tf_op jit(solution)/shard_map/all_to_all | solution.py:10
  345.1 237.5 %all-reduce.6.cloned.1.call-start = ((), (), s32[]{:S(2)}) async-start(), calls=%async_computation.3 | async-start | bytes 1048576 | tf_op jit(solution)/shard_map/psum | solution.py:49
  355.0 3.2 copy-start.3
  363.3 53.0 %collective-permute-start.2 = (f32[512,32]{0,1:T(8,128)S(1)}, f32[512,32]{0,1:T(8,128)S(1)}, u32[]{:S(2)}, u32[]{:S(2)}) collective-permute-start(f32[512,32]{0,1:T(8,128)S(1)} %fusion.42), channel_id=1, source_target_pairs={{0,16},{16,0},{8,24},{24,8},{32,48},{48,32},{40,56},{56,40},{64,80... | collective-permute-start | bytes 196616 | tf_op jit(solution)/shard_map/ppermute | solution.py:24
  503.7 241.2 %all-reduce.8.cloned.1.call-start = ((), (), s32[]{:S(2)}) async-start(), calls=%async_computation.4 | async-start | bytes 1048576 | tf_op jit(solution)/shard_map/psum | solution.py:49
  582.6 10.9 %collective-permute-start.3 = (f32[4096,32]{0,1:T(8,128)}, f32[4096,32]{0,1:T(8,128)S(1)}, u32[]{:S(2)}, u32[]{:S(2)}) collective-permute-start(f32[4096,32]{0,1:T(8,128)} %all-reduce.6.cloned.1.call-done), channel_id=1, source_target_pairs={{0,16},{16,0},{8,24},{24,8},{32,48},{48,32},{40,56},{56,40},{64,80... | collective-permute-start | bytes 1572872 | tf_op jit(solution)/shard_map/ppermute | solution.py:24
  602.9 3.2 copy-start.2
  611.2 4.4 collective-permute-start.4
  744.8 11.7 %collective-permute-start.5 = (f32[4096,32]{0,1:T(8,128)}, f32[4096,32]{0,1:T(8,128)S(1)}, u32[]{:S(2)}, u32[]{:S(2)}) collective-permute-start(f32[4096,32]{0,1:T(8,128)} %all-reduce.8.cloned.1.call-done), channel_id=1, source_target_pairs={{0,32},{32,0},{8,40},{40,8},{16,48},{48,16},{24,56},{56,24},{64,96... | collective-permute-start | bytes 1572872 | tf_op jit(solution)/shard_map/ppermute | solution.py:24
  746.4 10.2 %copy-start.8 = (f32[4096,32]{0,1:T(8,128)S(1)}, f32[4096,32]{0,1:T(8,128)}, u32[]{:S(2)}) copy-start(f32[4096,32]{0,1:T(8,128)} %all-reduce.8.cloned.1.call-done) | copy-start | bytes 1572868
  746.4 20.8 %copy-start.1 = (bf16[1,1024,512]{2,1,0:T(8,128)(2,1)S(1)}, bf16[1,1024,512]{2,1,0:T(8,128)(2,1)}, u32[]{:S(2)}) copy-start(bf16[1,1024,512]{2,1,0:T(8,128)(2,1)} %param.9) | copy-start | bytes 3145732
Sparse Core Ops, SparseCore 0:
  9.8 173.3 all-gather.1
  257.1 78.5 all-reduce.3
  503.8 78.7 all-reduce.5
  666.2 78.5 all-reduce.7
